TPU v7x, 128 devices: a whole 4x4x4 slice. The times are simulated.
128 devices in a mesh: dp: 32 (over y, x, core), blk: 4 (over z).
Axes of the slice: x: 4, y: 4, z: 4, core: 2. Of those that a mesh axis runs over, the one named last changes fastest.
Arguments:
- prod_feat: bfloat16 [32, 3072, 768], P('dp', 'blk'), may hold values from -23 to 23
- prec_feat: bfloat16 [32, 3072, 768], P('dp', 'blk'), may hold values from -23 to 23
- matched: int32 [32, 3072], P('dp', 'blk'), may hold values from 0 to 3071, each once within a row
- row_weight: float32 [32, 3072], P('dp', 'blk'), may hold values from 0.2 to 28, as said below
- proj_prod: bfloat16 [768, 1024], replicated, may hold values from -0.21875 to 0.21875
- proj_prec: bfloat16 [768, 1024], replicated, may hold values from -0.21875 to 0.21875
Outputs:
- loss_value: float32 [], replicated
- grad_prod: float32 [768, 1024], P('dp', 'blk')
- grad_prec: float32 [768, 1024], P('dp', 'blk')
Inputs may be any that keep to these rules, and one draw needn't show every extreme that they name: `matched`: in each of the 32 groups the 3072 values are a permutation of 0 to 3071. `row_weight`: positive.
All inputs are finite; a program needn't handle non-finite values.
Results may differ from a plain program's by a relative error of at most 0.0027.
Values may be sent and summed in bfloat16 or wider, within the bound.
No kernel may reach another device: no remote copies, remote signals or barrier semaphores. Data moves between devices by JAX's collectives and lax.ppermute only.
A program may use at most 128 MiB of HBM per device.

v0:
```python
import jax
import jax.numpy as jnp
from jax import lax
from jax.sharding import PartitionSpec as P

EPS = 1e-06
LOGIT_SCALE = 50.0


def embed_rows(features, weight):
    projected_raw = jnp.dot(features, weight, preferred_element_type=jnp.float32)
    radius = jnp.sqrt(jnp.sum(projected_raw * projected_raw, axis=1, keepdims=True) + EPS)
    unit_vec = projected_raw / radius
    return (unit_vec, unit_vec.astype(jnp.bfloat16), radius)


def similarity(queries, key_rows):
    return LOGIT_SCALE * lax.dot_general(
        queries, key_rows, (((1,), (1,)), ((), ())), preferred_element_type=jnp.float32
    )


def coefficient(scores, matches, weights, totals):
    probability = jnp.exp(scores - LOGIT_SCALE) / totals[:, None]
    return (weights[:, None] * (probability - matches.astype(jnp.float32))).astype(jnp.bfloat16)


def back_norm(unit_vec, radius, gradient):
    projected = jnp.sum(unit_vec * gradient, axis=1, keepdims=True)
    return ((gradient - unit_vec * projected) / radius).astype(jnp.bfloat16)


def spread_blocks(head, dp_size, blk_size):
    feat, embed = head.shape
    tiles = head.reshape(dp_size, feat // dp_size, blk_size, embed // blk_size)
    tiles = tiles.transpose(0, 2, 1, 3)
    return tiles.reshape(dp_size * blk_size * (feat // dp_size), embed // blk_size)


def per_device(prod_feat, prec_feat, matched, row_weight, proj_prod, proj_prec):
    feat_prod = prod_feat[0]
    feat_prec = prec_feat[0]
    targets = matched[0]
    weights = row_weight[0]
    dp_size = lax.axis_size("dp")
    blk_size = lax.axis_size("blk")
    unit_prod, unit16_prod, radius_prod = embed_rows(feat_prod, proj_prod)
    feat_prec_all = lax.all_gather(feat_prec, "blk", axis=0, tiled=True)
    unit_prec, unit16_prec, radius_prec = embed_rows(feat_prec_all, proj_prec)
    scores = similarity(unit16_prod, unit16_prec)
    columns = lax.iota(jnp.int32, unit16_prec.shape[0])
    matches = targets[:, None] == columns[None, :]
    totals = jnp.sum(jnp.exp(scores - LOGIT_SCALE), axis=1)
    positive = jnp.sum(jnp.where(matches, scores, 0.0), axis=1)
    losses = LOGIT_SCALE + jnp.log(totals) - positive
    loss_local = jnp.sum(weights * losses)
    weight_local = jnp.sum(weights)
    loss_sum, weight_total = lax.psum((loss_local, weight_local), ("dp", "blk"))
    coeffs = coefficient(scores, matches, weights, totals)
    grad_unit_prod = LOGIT_SCALE * jnp.dot(coeffs, unit16_prec, preferred_element_type=jnp.float32)
    grad_prec_part = LOGIT_SCALE * lax.dot_general(
        coeffs, unit16_prod, (((0,), (0,)), ((), ())), preferred_element_type=jnp.float32
    )
    dir_prod = back_norm(unit_prod, radius_prod, grad_unit_prod)
    dir_prec = back_norm(unit_prec, radius_prec, grad_prec_part)
    head_prod = lax.dot_general(
        feat_prod, dir_prod, (((0,), (0,)), ((), ())), preferred_element_type=jnp.float32
    )
    head_prec = lax.dot_general(
        feat_prec_all, dir_prec, (((0,), (0,)), ((), ())), preferred_element_type=jnp.float32
    )
    summed_prod = lax.psum_scatter(
        spread_blocks(head_prod, dp_size, blk_size), ("dp", "blk"), scatter_dimension=0, tiled=True
    )
    summed_prec = lax.psum_scatter(
        spread_blocks(head_prec, dp_size, blk_size), ("dp", "blk"), scatter_dimension=0, tiled=True
    )
    return (loss_sum / weight_total, summed_prod / weight_total, summed_prec / weight_total)


def solution(mesh):
    placed = (P("dp", "blk", None), P("dp", "blk", None), P("dp", "blk"), P("dp", "blk"), P(), P())
    return jax.shard_map(
        per_device,
        mesh=mesh,
        in_specs=placed,
        out_specs=(P(), P("dp", "blk"), P("dp", "blk")),
        check_vma=False,
    )
```

profile of v0, /device:TPU:0, one launch (start us, length us, event | category | flops | bytes accessed | tf_op | source)
XLA Modules:
  0.0 556.1 jit_solution(3797390125440202433)
XLA Ops:
  7.2 0.0 copy-start
  7.2 0.0 all-gather.3.cloned.1.call-start
  7.2 0.7 all-gather.3.cloned.1.call-update
  7.9 0.0 reduce-scatter.3.cloned.1.call-start
  8.0 0.7 reduce.2
  8.7 1.3 fusion.20
  10.0 4.8 multiply_reduce_fusion.3
  14.8 50.2 %all-gather.3.cloned.1.call-done = bf16[1,3072,768]{2,1,0:T(8,128)(2,1)} async-done(((bf16[1,768,768]{2,1,0:T(8,128)(2,1)}), bf16[1,3072,768]{2,1,0:T(8,128)(2,1)}) %all-gather.3.cloned.1.call-update) | async-done | bytes 4718608 | tf_op jit(solution)/shard_map/all_gather | solution.py:48
  65.0 0.0 copy-done
  65.0 0.0 copy-start.3
  65.0 7.4 %multiply_reduce_fusion.1 = (f32[3072]{0:T(1024)S(1)}, f32[3072,1024]{0,1:T(8,128)S(1)}) fusion(bf16[768,1024]{1,0:T(8,128)(2,1)S(1)} %copy-done, bf16[1,3072,768]{2,1,0:T(8,128)(2,1)} %all-gather.3.cloned.1.call-done), kind=kOutput, calls=%fused_computation.2 | convolution fusion | flops 4838126592 | bytes 18886656 | tf_op jit(solution)/shard_map/dot_general | solution.py:11
  72.4 0.0 copy-start.4
  72.4 0.0 copy-done.3
  72.4 9.7 %fusion = (f32[768]{0:T(1024)S(1)}, f32[768]{0:T(1024)S(1)}, f32[768,3072]{1,0:T(8,128)}) fusion(s32[768]{0:T(1024)S(1)} %reduce.2, f32[3072,1024]{0,1:T(8,128)S(1)} %get-tuple-element.12, f32[3072]{0:T(1024)S(1)} %add_sqrt_fusion, f32[768,1024]{1,0:T(8,128)S(1)} %copy-done.3, f32[768]{0:T(1024)S(1)} %add_sqrt_fusion.1), kind=kOutput, calls=%fused_computation.7 | convolution fusion | flops 4853856256 | bytes 25190400 | tf_op jit(solution)/shard_map/dot_general | solution.py:18
  82.2 0.0 copy-done.4
  82.2 13.6 %multiply_reduce_fusion.2 = (f32[768]{0:T(1024)S(1)}, f32[768,1024]{1,0:T(8,128)S(1)}) fusion(f32[768,1024]{1,0:T(8,128)S(1)} %copy-done.3, f32[768]{0:T(1024)S(1)} %add_sqrt_fusion.1, f32[3072,1024]{0,1:T(8,128)} %copy-done.4, f32[3072]{0:T(1024)S(1)} %add_sqrt_fusion, f32[768,3072]{1,0:T(8,128)} %get-tuple-element.13, f32[768]{0:T(1024)S(1)} %get-tuple-element.3, ...), kind=kOutput, calls=%fused_computation.14 | convolution fusion | flops 4860148736 | bytes 28339200 | tf_op jit(solution)/shard_map/dot_general | solution.py:60
  95.7 0.0 copy-start.2
  95.7 15.1 %multiply_reduce_fusion = (f32[3072]{0:T(1024)S(1)}, f32[3072,1024]{0,1:T(8,128)}) fusion(f32[3072,1024]{0,1:T(8,128)} %copy-done.4, f32[3072]{0:T(1024)S(1)} %add_sqrt_fusion, f32[768,1024]{1,0:T(8,128)S(1)} %copy-done.3, f32[768]{0:T(1024)S(1)} %add_sqrt_fusion.1, f32[768,3072]{1,0:T(8,128)} %get-tuple-element.13, f32[768]{0:T(1024)S(1)} %get-tuple-element.3, ...), kind=kOutput, calls=%fused_computation.1 | convolution fusion | flops 4864865280 | bytes 37785600 | tf_op jit(solution)/shard_map/dot_general | solution.py:61
  110.8 0.0 copy-done.2
  110.8 3.9 convolution_bitcast_fusion
  114.7 2.4 copy.13
  117.1 2.9 reshape.35
  120.0 4.2 copy.14
  124.3 0.0 reduce-scatter.3.cloned.1.call-update
  124.3 0.0 reduce-scatter.5.cloned.1.call-start
  124.3 12.6 %fusion.9 = f32[768,1024]{0,1:T(8,128)S(1)} fusion(bf16[1,3072,768]{2,1,0:T(8,128)(2,1)} %all-gather.3.cloned.1.call-done, f32[3072,1024]{0,1:T(8,128)} %get-tuple-element.17, f32[3072]{0:T(1024)S(1)} %get-tuple-element.16, f32[3072]{0:T(1024)S(1)} %add_sqrt_fusion, f32[3072,1024]{0,1:T(8,128)} %copy-done.4), kind=kOutput, calls=%fused_computation.20 | convolution fusion | flops 4850712576 | bytes 33054720 | tf_op jit(solution)/shard_map/dot_general | solution.py:69
  136.9 2.4 copy.15
  139.3 0.0 copy-start.1
  139.3 5.3 reshape.37
  144.6 4.2 copy.16
  148.7 0.0 reduce-scatter.5.cloned.1.call-update
  148.8 0.6 multiply_reduce_fusion.4
  149.4 64.6 %all-reduce = (f32[]{:T(128)}, f32[]{:T(128)}) all-reduce(f32[]{:T(128)} %multiply_reduce_fusion.4, f32[]{:T(128)} %get-tuple-element.5), channel_id=1, replica_groups=mesh['dp'=32,'blk'=4] {'dp','blk'}, use_global_device_ids=true, to_apply=%region_5.6 | all-reduce | flops 2 | bytes 16 | tf_op jit(solution)/shard_map/psum | solution.py:58
  215.4 119.1 %reduce-scatter.3.cloned.1.call-done = f32[24,256]{1,0:T(8,128)} async-done(((f32[3072,256]{1,0:T(8,128)}), f32[24,256]{1,0:T(8,128)}) %reduce-scatter.3.cloned.1.call-update) | async-done | bytes 24592 | tf_op jit(solution)/shard_map/reduce_scatter | solution.py:72
  334.5 2.0 broadcast_divide_fusion.3
  336.5 209.9 %reduce-scatter.5.cloned.1.call-done = f32[24,256]{1,0:T(8,128)} async-done(((f32[3072,256]{1,0:T(8,128)}), f32[24,256]{1,0:T(8,128)}) %reduce-scatter.5.cloned.1.call-update) | async-done | bytes 24592 | tf_op jit(solution)/shard_map/reduce_scatter | solution.py:75
  546.4 2.0 broadcast_divide_fusion.2
  548.4 0.0 copy-done.1
  (2 shorter events, 0.0 us)
Async XLA Ops:
  7.2 57.9 %copy-start = (bf16[768,1024]{1,0:T(8,128)(2,1)S(1)}, bf16[768,1024]{1,0:T(8,128)(2,1)}, u32[]{:S(2)}) copy-start(bf16[768,1024]{1,0:T(8,128)(2,1)} %param.11) | copy-start | bytes 4718596
  7.2 57.8 %all-gather.3.cloned.1.call-start = ((), (), s32[]{:S(2)}) async-start(), calls=%async_computation.4 | async-start | bytes 5898240 | tf_op jit(solution)/shard_map/all_gather | solution.py:48
  7.9 326.6 %reduce-scatter.3.cloned.1.call-start = ((), (), s32[]{:S(2)}) async-start(), calls=%async_computation.2 | async-start | bytes 3170304 | tf_op jit(solution)/shard_map/reduce_scatter | solution.py:72
  65.0 7.4 %copy-start.3 = (f32[768,1024]{1,0:T(8,128)S(1)}, f32[768,1024]{1,0:T(8,128)}, u32[]{:S(2)}) copy-start(f32[768,1024]{1,0:T(8,128)} %get-tuple-element.10) | copy-start | bytes 9437188
  72.4 9.8 %copy-start.4 = (f32[3072,1024]{0,1:T(8,128)}, f32[3072,1024]{0,1:T(8,128)S(1)}, u32[]{:S(2)}) copy-start(f32[3072,1024]{0,1:T(8,128)S(1)} %get-tuple-element.12) | copy-start | bytes 37748740
  95.7 15.1 %copy-start.2 = (bf16[1,768,768]{2,1,0:T(8,128)(2,1)S(1)}, bf16[1,768,768]{2,1,0:T(8,128)(2,1)}, u32[]{:S(2)}) copy-start(bf16[1,768,768]{2,1,0:T(8,128)(2,1)} %param.6) | copy-start | bytes 3538948
  124.3 422.1 %reduce-scatter.5.cloned.1.call-start = ((), (), s32[]{:S(2)}) async-start(), calls=%async_computation.3 | async-start | bytes 3170304 | tf_op jit(solution)/shard_map/reduce_scatter | solution.py:75
  139.3 409.2 %copy-start.1 = (bf16[768,1024]{1,0:T(8,128)(2,1)S(1)}, bf16[768,1024]{1,0:T(8,128)(2,1)}, u32[]{:S(2)}) copy-start(bf16[768,1024]{1,0:T(8,128)(2,1)} %param.11) | copy-start | bytes 4718596
Sparse Core Ops, SparseCore 0:
  9.7 55.3 all-gather.2
  124.4 210.0 reduce-scatter.2
  339.3 207.0 reduce-scatter.4
where the time goes:
time: 557 us; the launch traced here: 556 us
  waiting for transfers between devices  380 us (68%)
  matrix products  67 us (12%)
  blocking collectives  64.6 us (12%)
  local copies, waits for them, and re-layouts  21.4 us (4%)
  between operations  16.3 us (3%)
  other arithmetic  6.71 us (1%)
    reduce_scatter x1, waiting for transfers between devices, per_device(): lax.psum_scatter(spread_blocks(head_prec, dp_size, blk_size), ('dp', 'blk...  210 us
    reduce_scatter x1, waiting for transfers between devices, per_device(): lax.psum_scatter(spread_blocks(head_prod, dp_size, blk_size), ('dp', 'blk...  119 us
    psum x1, blocking collectives, per_device(): loss_sum, weight_total = lax.psum((loss_local, weight_local), ('dp', 'blk'))  64.6 us
    all_gather x1, waiting for transfers between devices, per_device(): feat_prec_all = lax.all_gather(feat_prec, 'blk', axis=0, tiled=True)  50.2 us
    dot_general x1, matrix products, per_device(): lax.dot_general(coeffs, unit16_prod, (((0,), (0,)), ((), ())), preferred_...  15.1 us
    dot_general x1, matrix products, per_device(): jnp.dot(coeffs, unit16_prec, preferred_element_type=jnp.float32)  13.6 us
    dot_general x1, matrix products, per_device(): lax.dot_general(feat_prec_all, dir_prec, (((0,), (0,)), ((), ())), prefer...  12.6 us
    dot_general x2, matrix products, embed_rows(): jnp.dot(features, weight, preferred_element_type=jnp.float32)  12.2 us
  transfers between devices with their start and end apart: 3, of which 3 were waited for; matrix products, arithmetic and copies ran while one was open for 6% of the time, Pallas kernels for 0%

commit v1 on v0

--- a/solution.py
+++ b/solution.py
@@ -2,6 +2,7 @@
 import jax.numpy as jnp
 from jax import lax
 from jax.sharding import PartitionSpec as P
+from jax.lax import all_to_all, axis_size
 
 EPS = 1e-06
 LOGIT_SCALE = 50.0
@@ -45,7 +46,9 @@
     dp_size = lax.axis_size("dp")
     blk_size = lax.axis_size("blk")
     unit_prod, unit16_prod, radius_prod = embed_rows(feat_prod, proj_prod)
-    feat_prec_all = lax.all_gather(feat_prec, "blk", axis=0, tiled=True)
+    feat_prec_all = jnp.concatenate(
+        all_to_all(jnp.stack([feat_prec for _ in range(axis_size("blk"))]), "blk", 0, 0), axis=0
+    )
     unit_prec, unit16_prec, radius_prec = embed_rows(feat_prec_all, proj_prec)
     scores = similarity(unit16_prod, unit16_prec)
     columns = lax.iota(jnp.int32, unit16_prec.shape[0])

time: 557 us -> 566 us (1.016)
  local copies, waits for them, and re-layouts: 21.4 us -> 29.9 us
    all_gather x1 -> x0, waiting for transfers between devices: 50.2 us -> none  [per_device(): feat_prec_all = lax.all_gather(feat_prec, 'blk', axis=0, tiled=True)]
    all_to_all x0 -> x1, waiting for transfers between devices: none -> 50.2 us  [per_device(): all_to_all(jnp.stack([feat_prec for _ in range(axis_size('blk'))]), 'blk'...]
where the time goes in v1:
time: 566 us; the launch traced here: 565 us
  waiting for transfers between devices  376 us (66%)
  matrix products  67.6 us (12%)
  blocking collectives  64.9 us (11%)
  local copies, waits for them, and re-layouts  29.9 us (5%)
  between operations  16.6 us (3%)
    reduce_scatter x1, waiting for transfers between devices, per_device(): lax.psum_scatter(spread_blocks(head_prec, dp_size, blk_size), ('dp', 'blk...  210 us
    reduce_scatter x1, waiting for transfers between devices, per_device(): lax.psum_scatter(spread_blocks(head_prod, dp_size, blk_size), ('dp', 'blk...  116 us
    psum x1, blocking collectives, per_device(): loss_sum, weight_total = lax.psum((loss_local, weight_local), ('dp', 'blk'))  64.9 us
    all_to_all x1, waiting for transfers between devices, per_device(): all_to_all(jnp.stack([feat_prec for _ in range(axis_size('blk'))]), 'blk'...  50.2 us
    dot_general x1, matrix products, per_device(): lax.dot_general(coeffs, unit16_prod, (((0,), (0,)), ((), ())), preferred_...  15.1 us
    dot_general x1, matrix products, per_device(): lax.dot_general(feat_prec_all, dir_prec, (((0,), (0,)), ((), ())), prefer...  13.7 us
    dot_general x1, matrix products, per_device(): jnp.dot(coeffs, unit16_prec, preferred_element_type=jnp.float32)  13.6 us
    dot_general x2, matrix products, embed_rows(): jnp.dot(features, weight, preferred_element_type=jnp.float32)  11.7 us
  transfers between devices with their start and end apart: 3, of which 3 were waited for; matrix products, arithmetic and copies ran while one was open for 6% of the time, Pallas kernels for 0%

profile of v1, /device:TPU:0, one launch (start us, length us, event | category | flops | bytes accessed | tf_op | source)
XLA Modules:
  0.0 565.3 jit_solution(15258442012262144938)
XLA Ops:
  7.2 0.0 copy-start
  7.2 0.0 copy-start.2
  7.2 0.0 copy-start.3
  7.2 0.0 copy-start.4
  7.2 3.8 stack.3
  11.1 5.4 all-to-all-start
  16.5 0.0 reduce-scatter.3.cloned.1.call-start
  16.5 0.0 copy-done.2
  16.5 0.0 copy-done.3
  16.5 0.6 fusion.15
  17.1 0.0 copy-done.4
  17.1 4.3 multiply_reduce_fusion.3
  21.4 50.2 %all-to-all-done = bf16[4,768,768]{2,1,0:T(8,128)(2,1)} async-done(((bf16[4,768,768]{2,1,0:T(8,128)(2,1)}), bf16[4,768,768]{2,1,0:T(8,128)(2,1)}, u32[]{:S(2)}, u32[]{:S(2)}) %all-to-all-start) | async-done | bytes 4718624 | tf_op jit(solution)/shard_map/all_to_all | solution.py:50
  71.7 0.0 copy-done
  71.7 0.0 copy-start.6
  71.7 7.4 %multiply_reduce_fusion.1 = (f32[3072]{0:T(1024)S(1)}, f32[3072,1024]{0,1:T(8,128)S(1)}) fusion(bf16[3072,768]{1,0:T(8,128)(2,1)} %bitcast.2, bf16[768,1024]{1,0:T(8,128)(2,1)S(1)} %copy-done), kind=kOutput, calls=%fused_computation.2 | convolution fusion | flops 4838126592 | bytes 18886656 | tf_op jit(solution)/shard_map/dot_general | solution.py:12
  79.0 0.0 copy-start.7
  79.1 0.0 copy-done.6
  79.1 9.7 %fusion = (f32[768]{0:T(1024)S(1)}, f32[768]{0:T(1024)S(1)}, f32[768,3072]{1,0:T(8,128)}) fusion(s32[768]{0:T(1024)S(1)} %reduce.2, f32[3072,1024]{0,1:T(8,128)S(1)} %get-tuple-element.12, f32[3072]{0:T(1024)S(1)} %add_sqrt_fusion, f32[768,1024]{1,0:T(8,128)S(1)} %copy-done.6, f32[768]{0:T(1024)S(1)} %add_sqrt_fusion.1), kind=kOutput, calls=%fused_computation.7 | convolution fusion | flops 4853856256 | bytes 25190400 | tf_op jit(solution)/shard_map/dot_general | solution.py:19
  88.8 0.0 copy-done.7
  88.8 13.6 %multiply_reduce_fusion.2 = (f32[768]{0:T(1024)S(1)}, f32[768,1024]{1,0:T(8,128)S(1)}) fusion(f32[768,1024]{1,0:T(8,128)S(1)} %copy-done.6, f32[768]{0:T(1024)S(1)} %add_sqrt_fusion.1, f32[3072,1024]{0,1:T(8,128)} %copy-done.7, f32[3072]{0:T(1024)S(1)} %add_sqrt_fusion, f32[768,3072]{1,0:T(8,128)} %get-tuple-element.13, f32[768]{0:T(1024)S(1)} %get-tuple-element.3, ...), kind=kOutput, calls=%fused_computation.11 | convolution fusion | flops 4860148736 | bytes 28339200 | tf_op jit(solution)/shard_map/dot_general | solution.py:63
  102.3 0.0 copy-start.5
  102.3 15.1 %multiply_reduce_fusion = (f32[3072]{0:T(1024)S(1)}, f32[3072,1024]{0,1:T(8,128)}) fusion(f32[3072,1024]{0,1:T(8,128)} %copy-done.7, f32[3072]{0:T(1024)S(1)} %add_sqrt_fusion, f32[768,1024]{1,0:T(8,128)S(1)} %copy-done.6, f32[768]{0:T(1024)S(1)} %add_sqrt_fusion.1, f32[768,3072]{1,0:T(8,128)} %get-tuple-element.13, f32[768]{0:T(1024)S(1)} %get-tuple-element.3, ...), kind=kOutput, calls=%fused_computation.1 | convolution fusion | flops 4864865280 | bytes 37785600 | tf_op jit(solution)/shard_map/dot_general | solution.py:64
  117.4 0.0 copy-done.5
  117.4 3.8 convolution_bitcast_fusion
  121.3 3.6 copy.13
  124.9 5.1 reshape.40
  130.0 4.2 copy.14
  134.3 0.0 reduce-scatter.3.cloned.1.call-update
  134.3 0.0 reduce-scatter.5.cloned.1.call-start
  134.3 13.7 %fusion.6 = f32[768,1024]{0,1:T(8,128)} fusion(bf16[3072,768]{1,0:T(8,128)(2,1)} %bitcast.2, f32[3072,1024]{0,1:T(8,128)} %get-tuple-element.17, f32[3072]{0:T(1024)S(1)} %get-tuple-element.16, f32[3072]{0:T(1024)S(1)} %add_sqrt_fusion, f32[3072,1024]{0,1:T(8,128)} %copy-done.7), kind=kOutput, calls=%fused_computation.17 | convolution fusion | flops 4850712576 | bytes 33054720 | tf_op jit(solution)/shard_map/dot_general | solution.py:72
  148.0 3.6 copy.15
  151.6 0.0 copy-start.1
  151.6 5.3 reshape.42
  156.9 4.2 copy.16
  161.1 0.0 reduce-scatter.5.cloned.1.call-update
  161.1 0.6 multiply_reduce_fusion.4
  161.7 64.9 %all-reduce = (f32[]{:T(128)}, f32[]{:T(128)}) all-reduce(f32[]{:T(128)} %multiply_reduce_fusion.4, f32[]{:T(128)} %get-tuple-element.5), channel_id=1, replica_groups=mesh['dp'=32,'blk'=4] {'dp','blk'}, use_global_device_ids=true, to_apply=%region_5.6 | all-reduce | flops 2 | bytes 16 | tf_op jit(solution)/shard_map/psum | solution.py:61
  227.9 115.5 %reduce-scatter.3.cloned.1.call-done = f32[24,256]{1,0:T(8,128)} async-done(((f32[3072,256]{1,0:T(8,128)}), f32[24,256]{1,0:T(8,128)}) %reduce-scatter.3.cloned.1.call-update) | async-done | bytes 24592 | tf_op jit(solution)/shard_map/reduce_scatter | solution.py:75
  343.4 2.0 broadcast_divide_fusion.3
  345.4 209.9 %reduce-scatter.5.cloned.1.call-done = f32[24,256]{1,0:T(8,128)} async-done(((f32[3072,256]{1,0:T(8,128)}), f32[24,256]{1,0:T(8,128)}) %reduce-scatter.5.cloned.1.call-update) | async-done | bytes 24592 | tf_op jit(solution)/shard_map/reduce_scatter | solution.py:78
  555.3 2.0 broadcast_divide_fusion.2
  557.3 0.0 copy-done.1
  (3 shorter events, 0.0 us)
Async XLA Ops:
  7.2 64.5 %copy-start = (bf16[768,1024]{1,0:T(8,128)(2,1)S(1)}, bf16[768,1024]{1,0:T(8,128)(2,1)}, u32[]{:S(2)}) copy-start(bf16[768,1024]{1,0:T(8,128)(2,1)} %param.11) | copy-start | bytes 4718596
  7.2 9.3 %copy-start.2 = (s32[1,768]{1,0:T(1,128)S(1)}, s32[1,768]{1,0:T(1,128)}, u32[]{:S(2)}) copy-start(s32[1,768]{1,0:T(1,128)} %param.8) | copy-start | bytes 9220
  7.2 9.3 %copy-start.3 = (f32[1,768]{1,0:T(1,128)S(1)}, f32[1,768]{1,0:T(1,128)}, u32[]{:S(2)}) copy-start(f32[1,768]{1,0:T(1,128)} %param.9) | copy-start | bytes 9220
  7.2 9.9 %copy-start.4 = (bf16[768,1024]{1,0:T(8,128)(2,1)S(1)}, bf16[768,1024]{1,0:T(8,128)(2,1)}, u32[]{:S(2)}) copy-start(bf16[768,1024]{1,0:T(8,128)(2,1)} %param.10) | copy-start | bytes 4718596
  11.1 60.6 %all-to-all-start = ((bf16[4,768,768]{2,1,0:T(8,128)(2,1)}), bf16[4,768,768]{2,1,0:T(8,128)(2,1)}, u32[]{:S(2)}, u32[]{:S(2)}) async-start(bf16[4,768,768]{2,1,0:T(8,128)(2,1)} %stack.3), calls=%async_computation | async-start | bytes 9437184 | tf_op jit(solution)/shard_map/all_to_all | solution.py:50
  16.5 327.0 %reduce-scatter.3.cloned.1.call-start = ((), (), s32[]{:S(2)}) async-start(), calls=%async_computation.3 | async-start | bytes 3170304 | tf_op jit(solution)/shard_map/reduce_scatter | solution.py:75
  71.7 7.4 %copy-start.6 = (f32[768,1024]{1,0:T(8,128)S(1)}, f32[768,1024]{1,0:T(8,128)}, u32[]{:S(2)}) copy-start(f32[768,1024]{1,0:T(8,128)} %get-tuple-element.10) | copy-start | bytes 9437188
  79.0 9.7 %copy-start.7 = (f32[3072,1024]{0,1:T(8,128)}, f32[3072,1024]{0,1:T(8,128)S(1)}, u32[]{:S(2)}) copy-start(f32[3072,1024]{0,1:T(8,128)S(1)} %get-tuple-element.12) | copy-start | bytes 37748740
  102.3 15.1 %copy-start.5 = (bf16[1,768,768]{2,1,0:T(8,128)(2,1)S(1)}, bf16[1,768,768]{2,1,0:T(8,128)(2,1)}, u32[]{:S(2)}) copy-start(bf16[1,768,768]{2,1,0:T(8,128)(2,1)} %param.6) | copy-start | bytes 3538948
  134.3 421.0 %reduce-scatter.5.cloned.1.call-start = ((), (), s32[]{:S(2)}) async-start(), calls=%async_computation.4 | async-start | bytes 3170304 | tf_op jit(solution)/shard_map/reduce_scatter | solution.py:78
  151.6 405.7 %copy-start.1 = (bf16[768,1024]{1,0:T(8,128)(2,1)S(1)}, bf16[768,1024]{1,0:T(8,128)(2,1)}, u32[]{:S(2)}) copy-start(bf16[768,1024]{1,0:T(8,128)(2,1)} %param.11) | copy-start | bytes 4718596
Sparse Core Ops, SparseCore 0:
  134.4 208.9 reduce-scatter.2
  348.2 207.0 reduce-scatter.4
